TPU v7x, 128 devices: a whole 4x4x4 slice. The times are simulated.
128 devices in a mesh: seq: 32 (over x, z, core), tp: 4 (over y).
Axes of the slice: x: 4, y: 4, z: 4, core: 2. Of those that a mesh axis runs over, the one named last changes fastest.
Arguments:
- tokens: bfloat16 [8192, 2048], P('seq'), may hold values from -6 to 6
- norm_gain: float32 [2048], replicated, may hold values from 0.1 to 1.9
- qkv_weight: bfloat16 [2048, 4096], P(None, 'tp'), may hold values from -0.125 to 0.125
- conv_weight: float32 [4, 4096], P(None, 'tp'), may hold values from -3 to 3
- gate_down: bfloat16 [2048, 16], replicated, may hold values from -0.125 to 0.125
- gate_up: bfloat16 [16, 1024], P(None, 'tp'), may hold values from -6 to 6
- gate_bias: float32 [1024], P('tp'), may hold values from 0.3 to 8.5
- out_gate_weight: bfloat16 [2048, 2048], P(None, 'tp'), may hold values from -0.125 to 0.125
- head_gain: float32 [512], replicated, may hold values from 0.1 to 1.9
- out_weight: bfloat16 [2048, 2048], P('tp'), may hold values from -0.125 to 0.125
- final_gain: float32 [2048], replicated, may hold values from 0.1 to 1.9
- embedding: bfloat16 [32000, 2048], P(('seq', 'tp')), may hold values from -0.5 to 0.5
- lengths: int32 [8], replicated, may hold values from 1 to 4096, as said below
- packed_order: int32 [8], replicated, may hold values from 0 to 7, each once
Outputs:
- hidden: bfloat16 [8192, 2048], P('seq', 'tp')
- last_states: float32 [8, 4, 256, 512], P(None, 'tp')
- conv_edges: float32 [8, 3, 4096], P(None, None, 'tp')
- last_norms: float32 [8], replicated
- max_logits: float32 [8, 128], P(None, ('seq', 'tp'))
Inputs may be any that keep to these rules, and one draw needn't show every extreme that they name: Request r of the initial order has lengths[r] tokens; the lengths sum to 8192, the largest is 4096 and the smallest is 1 or 2. packed_order names every request once; the packed positions hold the tokens of request packed_order[0], then those of packed_order[1], and so on.
All inputs are finite; a program needn't handle non-finite values.
Results may differ from a plain program's by a relative error of at most 0.015.
Values may be sent and summed in bfloat16 or wider, within the bound.
No kernel may reach another device: no remote copies, remote signals or barrier semaphores. Data moves between devices by JAX's collectives and lax.ppermute only.
A program may use at most 128 MiB of HBM per device.

v0:
```python
from functools import partial
import jax
import jax.numpy as jnp
from jax import lax
from jax.sharding import PartitionSpec as P

DK = 256
DV = 512
KCONV = 4
BLOCK = 64
HIGHEST_PRECISION = lax.Precision.HIGHEST


def prefix(array, axis, combine, identity):
    peers, place = (lax.axis_size(axis), lax.axis_index(axis))
    everything = jax.tree.map(
        lambda part, kind: lax.all_gather(part.astype(kind), axis),
        array,
        (jnp.bfloat16, jnp.bfloat16),
    )
    start = jax.tree.map(
        lambda part, zero: jnp.broadcast_to(jnp.asarray(zero, part.dtype), part.shape),
        array,
        identity,
    )

    def hop(k, before):
        reached = k < place
        new = combine(
            before, jax.tree.map(lambda part, own: part[k].astype(own.dtype), everything, array)
        )
        return jax.tree.map(lambda a, b: jnp.where(reached, a, b), new, before)

    return lax.fori_loop(0, peers, hop, start)


def passed_along(array, axis, by):
    peers = lax.axis_size(axis)
    pairs = [(i, i + by) for i in range(peers) if 0 <= i + by < peers]
    return lax.ppermute(array, axis, pairs)


def segments(lengths, packed_order, positions):
    request_count = lengths.shape[0]
    select = (packed_order[:, None] == jnp.arange(request_count, dtype=jnp.int32)[None, :]).astype(
        jnp.int32
    )
    packed_len = jnp.sum(select * lengths[None, :], axis=1)
    end_points = jnp.cumsum(packed_len)
    starts = end_points - packed_len
    segment = jnp.sum((positions[:, None] >= starts[None, :]).astype(jnp.int32), axis=1) - 1
    last_index = jnp.sum(select * (end_points - 1)[:, None], axis=0)
    return (segment, last_index)


def causal_conv(padded, padded_segment, conv_weight, row_count):
    running = jnp.zeros((row_count, padded.shape[1]), jnp.float32)
    current = padded_segment[KCONV - 1 :]
    for offset in range(KCONV):
        window = padded[offset : offset + row_count]
        same_segment = (padded_segment[offset : offset + row_count] == current)[:, None]
        running = running + jnp.where(same_segment, window, 0.0) * conv_weight[offset]
    return running


def activate(convolved, head_count):
    shaped = convolved.reshape(convolved.shape[0], head_count, 2 * DK + DV)
    channel = jnp.arange(2 * DK + DV)
    return jnp.where(channel < 2 * DK, jax.nn.silu(shaped), shaped).astype(jnp.bfloat16)


def advance(carry_state, key_floats, values, cumulative, segment, segment_before):
    total_decay = cumulative[-1]
    same_tail = (segment == segment[-1])[:, None, None]
    scaled = jnp.where(same_tail, key_floats * jnp.exp(total_decay[None] - cumulative), 0.0).astype(
        jnp.bfloat16
    )
    added = jnp.einsum("jhc,jhv->hcv", scaled, values, preferred_element_type=jnp.float32)
    through = segment[-1] == segment_before
    return jnp.where(through, jnp.exp(total_decay)[:, :, None] * carry_state, 0.0) + added


def state_at_ends(
    end_states, carry_state, key_floats, values, cumulative, segment, segment_before, offset
):
    length = segment.shape[0]
    inside_block = (offset >= 0) & (offset < length)

    def add_ends(previous):
        end_row = jnp.clip(offset, 0, length - 1)
        end_decay = cumulative[end_row]
        end_segment = segment[end_row]
        indices = jnp.arange(length)
        allowed = (
            (indices[None, :] <= end_row[:, None]) & (segment[None, :] == end_segment[:, None])
        )[:, :, None, None]
        spread = jnp.where(allowed, end_decay[:, None] - cumulative[None], 0.0)
        weighted = jnp.where(allowed, key_floats[None] * jnp.exp(spread), 0.0).astype(jnp.bfloat16)
        within = jnp.einsum("rjhc,jhv->rhcv", weighted, values, preferred_element_type=jnp.float32)
        carried = (end_segment == segment_before)[:, None, None, None]
        reached = jnp.where(carried, jnp.exp(end_decay)[:, :, :, None] * carry_state[None], 0.0)
        return jnp.where(inside_block[:, None, None, None], within + reached, previous)

    def keep(previous):
        return previous

    return lax.cond(jnp.any(inside_block), add_ends, keep, end_states)


def block_step(last_index, carry, inputs):
    carry_state, end_states = carry
    queries, key_rows, values, decays, segment, segment_before, block_first = inputs
    cumulative = jnp.cumsum(decays, axis=0)
    length = segment.shape[0]
    indices = jnp.arange(length)
    causal = (indices[None, :] <= indices[:, None]) & (segment[None, :] == segment[:, None])
    allowed = causal[:, :, None, None]
    spread = jnp.where(allowed, cumulative[:, None] - cumulative[None, :], 0.0)
    weights = jnp.where(allowed, jnp.exp(spread), 0.0)
    query_rows = queries.astype(jnp.float32)
    key_floats = key_rows.astype(jnp.float32)
    scores = jnp.sum(query_rows[:, None] * key_floats[None, :] * weights, axis=-1).astype(
        jnp.bfloat16
    )
    inside = jnp.einsum("ijh,jhv->ihv", scores, values, preferred_element_type=jnp.float32)
    carried = (segment == segment_before)[:, None, None]
    outside = jnp.einsum(
        "ihc,hcv->ihv", query_rows * jnp.exp(cumulative), carry_state, precision=HIGHEST_PRECISION
    )
    output = inside + jnp.where(carried, outside, 0.0)
    new_state = advance(carry_state, key_floats, values, cumulative, segment, segment_before)
    end_states = state_at_ends(
        end_states,
        carry_state,
        key_floats,
        values,
        cumulative,
        segment,
        segment_before,
        last_index - block_first,
    )
    return ((new_state, end_states), output)


def state_only(carry_state, inputs):
    block_queries, block_keys, block_values, block_decays, block_segment, before, block_start = (
        inputs
    )
    cumulative = jnp.cumsum(block_decays, axis=0)
    return (
        advance(
            carry_state,
            block_keys.astype(jnp.float32),
            block_values,
            cumulative,
            block_segment,
            before,
        ),
        None,
    )


def head_output(attended, gate_out, head_gain):
    row_count, head_count, value_width = attended.shape
    mean_square = jnp.mean(attended * attended, axis=2, keepdims=True)
    gate_values = jax.nn.silu(
        gate_out.astype(jnp.float32).reshape(row_count, head_count, value_width)
    )
    gated = attended * lax.rsqrt(mean_square + 1e-05) * head_gain * gate_values
    return gated.reshape(row_count, head_count * value_width).astype(jnp.bfloat16)


def carry_in(decay_factor, local_state):

    def combine(earlier, later):
        return (earlier[0] * later[0], later[0][:, :, None] * earlier[1] + later[1])

    identity = (jnp.ones_like(decay_factor), jnp.zeros_like(local_state))
    result = prefix((decay_factor, local_state), "seq", combine, identity)
    return result[1]


def shards(
    tokens,
    norm_gain,
    qkv_weight,
    conv_weight,
    gate_down,
    gate_up,
    gate_bias,
    out_gate_weight,
    head_gain,
    out_weight,
    final_gain,
    embedding,
    lengths,
    packed_order,
):
    row_count = tokens.shape[0]
    head_count = out_weight.shape[0] // DV
    column_count = tokens.shape[1] // lax.axis_size("tp")
    start_row = lax.axis_index("seq") * row_count
    positions = start_row + jnp.arange(-(KCONV - 1), row_count, dtype=jnp.int32)
    segment_all, last_index = segments(lengths, packed_order, positions)
    segment = segment_all[KCONV - 1 :]
    segment_prior = segment_all[KCONV - 2]
    first_index = last_index - lengths + 1
    residual = tokens.astype(jnp.float32)
    normed = (
        residual
        * lax.rsqrt(jnp.mean(residual * residual, axis=1, keepdims=True) + 1e-06)
        * norm_gain
    ).astype(jnp.bfloat16)
    projected = jnp.dot(normed, qkv_weight, preferred_element_type=jnp.float32).astype(jnp.bfloat16)
    rim_rows = passed_along(projected[row_count - (KCONV - 1) :], "seq", 1)
    padded = jnp.concatenate([rim_rows, projected], axis=0)
    convolved = causal_conv(padded.astype(jnp.float32), segment_all, conv_weight, row_count)
    activated = activate(convolved, head_count)
    queries = activated[:, :, :DK]
    key_rows = activated[:, :, DK : 2 * DK]
    values = activated[:, :, 2 * DK :]
    lowrank = jnp.dot(normed, gate_down, preferred_element_type=jnp.float32)
    gate_logits = (
        jnp.dot(lowrank, gate_up.astype(jnp.float32), precision=HIGHEST_PRECISION) + gate_bias
    )
    decays = (jax.nn.log_sigmoid(gate_logits) / 16.0).reshape(row_count, head_count, DK)
    gate_out = jnp.dot(normed, out_gate_weight, preferred_element_type=jnp.float32).astype(
        jnp.bfloat16
    )
    block_count = row_count // BLOCK

    def split_blocks(array):
        return array.reshape((block_count, BLOCK) + array.shape[1:])

    segment_before = segment_all[KCONV - 2 : KCONV - 2 + row_count : BLOCK]
    block_first = start_row + jnp.arange(block_count, dtype=jnp.int32) * BLOCK
    block_inputs = (
        split_blocks(queries),
        split_blocks(key_rows),
        split_blocks(values),
        split_blocks(decays),
        split_blocks(segment),
        segment_before,
        block_first,
    )
    through_shard = segment[-1] == segment_prior
    empty_state = jnp.zeros((head_count, DK, DV), jnp.float32)
    empty_ends = jnp.zeros((lengths.shape[0], head_count, DK, DV), jnp.float32)
    stepper = partial(block_step, last_index)
    local_state, unused_steps = lax.scan(state_only, empty_state, block_inputs)
    decay_factor = jnp.where(through_shard, jnp.exp(jnp.sum(decays, axis=0)), 0.0)
    incoming = carry_in(decay_factor, local_state)
    (unused_state, end_states), attended = lax.scan(stepper, (incoming, empty_ends), block_inputs)
    attended = attended.reshape(row_count, head_count, DV)
    gated = head_output(attended, gate_out, head_gain)
    projected_out = jnp.dot(gated, out_weight, preferred_element_type=jnp.float32)
    summed = lax.psum_scatter(
        projected_out.astype(jnp.bfloat16), "tp", scatter_dimension=1, tiled=True
    ).astype(jnp.float32)
    column_start = lax.axis_index("tp") * column_count
    own_columns = lax.dynamic_slice_in_dim(residual, column_start, column_count, 1)
    hidden = (own_columns + summed).astype(jnp.bfloat16)
    owned_here = (last_index >= start_row) & (last_index < start_row + row_count)
    local_last = jnp.clip(last_index - start_row, 0, row_count - 1)
    last_rows = jnp.where(owned_here[:, None], hidden[local_last].astype(jnp.float32), 0.0)
    edge_list = []
    for offset in range(KCONV - 1):
        located = last_index - (KCONV - 2) + offset
        inside = owned_here & (located >= first_index)
        picked = padded[jnp.clip(located - start_row + KCONV - 1, 0, row_count + KCONV - 2)].astype(
            jnp.float32
        )
        edge_list.append(jnp.where(inside[:, None], picked, 0.0))
    conv_edges = jnp.stack(edge_list, axis=1)
    row_sums, conv_edges, last_states = (
        lax.psum(last_rows.astype(jnp.bfloat16), "seq").astype(jnp.float32),
        lax.psum(conv_edges.astype(jnp.bfloat16), "seq").astype(jnp.float32),
        lax.psum(end_states.astype(jnp.bfloat16), "seq").astype(jnp.float32),
    )
    full_rows = lax.all_gather(row_sums, "tp", axis=1, tiled=True)
    mean_square = jnp.mean(full_rows * full_rows, axis=1)
    last_norms = jnp.sqrt(mean_square)
    final_rows = (full_rows * lax.rsqrt(mean_square[:, None] + 1e-06) * final_gain).astype(
        jnp.bfloat16
    )
    logits = jnp.dot(final_rows, embedding.T, preferred_element_type=jnp.float32)
    max_logits = jnp.max(logits, axis=1, keepdims=True)
    return (hidden, last_states, conv_edges, last_norms, max_logits)


def solution(mesh):
    in_specs = (
        P("seq", None),
        P(),
        P(None, "tp"),
        P(None, "tp"),
        P(),
        P(None, "tp"),
        P("tp"),
        P(None, "tp"),
        P(),
        P("tp", None),
        P(),
        P(("seq", "tp"), None),
        P(),
        P(),
    )
    out_specs = (
        P("seq", "tp"),
        P(None, "tp", None, None),
        P(None, None, "tp"),
        P(),
        P(None, ("seq", "tp")),
    )
    return jax.shard_map(shards, mesh=mesh, in_specs=in_specs, out_specs=out_specs, check_vma=False)
```

profile of v0, /device:TPU:0, one launch (start us, length us, event | category | flops | bytes accessed | tf_op | source)
XLA Modules:
  0.0 477.1 jit_solution(16728195551736005816)
XLA Ops:
  7.2 1.6 multiply_reduce_fusion.1
  9.0 3.9 convolution_convert_fusion.1
  12.9 1.3 collective-permute-start
  14.8 1.7 fusion.70
  21.1 21.8 %while.43 = (s32[]{:T(128)}, f32[1,256,512]{2,1,0:T(8,128)S(1)}, s32[4,64]{1,0:T(4,128)S(1)}, s32[4]{0:T(128)S(1)}, f32[4,64,1,256]{3,2,1,0:T(1,128)}, /*index=5...) while((s32[]{:T(128)}, f32[1,256,512]{2,1,0:T(8,128)S(1)}, ...), condition=%wide.region_7.8_spmd.clone, body=%wide.region_5.7_spmd.clone.sunk | while | flops 18415684 | bytes 1417237 | solution.py:250
  25.3 1.2 fusion.123
  30.8 1.2 fusion.123
  36.2 1.2 fusion.123
  41.7 1.2 fusion.123
  45.5 26.3 %all-gather.2 = bf16[32,1,256]{2,1,0:T(2,128)(2,1)S(1)} all-gather(bf16[1,1,256]{2,1,0:T(2,128)(2,1)S(1)} %reshape.975), channel_id=2, replica_groups=mesh['seq'=32,'tp'=4] {'seq'}, dimensions={0}, use_global_device_ids=true | all-gather | bytes 16896 | tf_op jit(solution)/shard_map/all_gather | solution.py:17
  71.9 29.0 %all-gather.5.cloned.1.call-done = bf16[32,256,512]{2,1,0:T(8,128)(2,1)} async-done(((bf16[1,256,512]{2,1,0:T(8,128)(2,1)}), bf16[32,256,512]{2,1,0:T(8,128)(2,1)}) %all-gather.5.cloned.1.call-update) | async-done | bytes 8388624 | tf_op jit(solution)/shard_map/all_gather | solution.py:17
  101.0 36.2 %while.44 = (s32[]{:T(128)}, f32[1,256,512]{2,1,0:T(8,128)S(1)}, s32[]{:T(128)}, bf16[32,1,256]{2,1,0:T(2,128)(2,1)S(1)}, bf16[32,1,256,512]{3,2,1,0:T(8,128)(2,1)}, /*index=5*/s32[]{:T(128)}, s32[]{:T(128)}) while((s32[]{:T(128)}, f32[1,256,512]{2,1,0:T(8,128)S(1)}, s32[]{:T(128)}, bf16[32,1,256]{2,1,0:T(2,128)(2,1)S(1)}, ...), condition=%wide.region_9.10_spmd.clone, body=%wide.region_8.9_spmd.clone.sunk | while | flops 655620 | bytes 1313385 | solution.py:34
  102.1 1.1 fusion.124
  103.2 1.1 fusion.124
  137.1 1.5 broadcast_in_dim.240
  138.6 54.6 %while.42 = (s32[]{:T(128)}, f32[1,256,512]{2,1,0:T(8,128)S(1)}, bf16[8,1,256,512]{3,2,0,1:T(8,128)(2,1)}, f32[4,64,1,512]{3,1,2,0:T(8,128)}, s32[4,64]{1,0:T(4,...) while((s32[]{:T(128)}, f32[1,256,512]{2,1,0:T(8,128)S(1)}, ...), condition=%wide.region_17.18_spmd, body=%wide.region_11.17_spmd.sunk | while | flops 268659424 | bytes 8804605 | solution.py:253
  144.4 5.7 %conditional.2 = (bf16[8,1,256,512]{3,2,0,1:T(8,128)(2,1)}) conditional(s32[]{:T(128)} %convert_element_type.388, bf16[8,1,256,512]{3,2,0,1:T(8,128)(2,1)} %get-tuple-element.722, (pred[8]{0:T(512)(128)(4,1)S(1)}, s32[8]{0:T(128)S(1)}, s32[64]{0:T(128)S(1)}, bf16[1,64,1,256]{3,2,1,0:T(2,128)(2,1)S(1)}, f32[64,1,256]{2,1,0:T(1,128)S(1)}, ...), branch_computations={%region_14.14_spmd, %region_15.15_spmd} | conditional | flops 139086368 | bytes 5199492 | solution.py:107
  146.4 3.7 fusion
  150.3 2.0 multiply_reduce_fusion.5
  162.5 2.0 multiply_reduce_fusion.5
  174.7 2.0 multiply_reduce_fusion.5
  187.0 2.0 multiply_reduce_fusion.5
  194.5 2.8 fusion.56
  197.3 1.7 convolution_convert_fusion
  199.0 2.8 convert_element_type.287
  203.9 96.7 %all-reduce.3.cloned.1.call-done = bf16[8,1,256,512]{3,2,1,0:T(8,128)(2,1)} async-done(((bf16[8,1,256,512]{3,2,1,0:T(8,128)(2,1)}), bf16[8,1,256,512]{3,2,1,0:T(8,128)(2,1)}) %all-reduce.3.cloned.1.call-update) | async-done | bytes 2097168 | tf_op jit(solution)/shard_map/psum | solution.py:278
  300.6 4.2 convert_element_type.304
  304.8 21.7 %reduce-scatter.2.cloned.1.call-done = bf16[256,512]{1,0:T(8,128)(2,1)} async-done(((bf16[256,2048]{1,0:T(8,128)(2,1)}), bf16[256,512]{1,0:T(8,128)(2,1)}) %reduce-scatter.2.cloned.1.call-update) | async-done | bytes 262160 | tf_op jit(solution)/shard_map/reduce_scatter | solution.py:257
  326.5 1.2 add_convert_fusion
  328.3 126.8 %all-reduce = (bf16[8,3,1024]{2,0,1:T(8,128)(2,1)S(1)}, bf16[8,512]{1,0:T(8,128)(2,1)S(1)}) all-reduce(bf16[8,3,1024]{2,0,1:T(8,128)(2,1)S(1)} %pad_maximum_fusion.1, bf16[8,512]{1,0:T(8,128)(2,1)S(1)} %select_convert_fusion.2), channel_id=1, replica_groups=mesh['seq'=32,'tp'=4] {'seq'}, use_global_device_ids=true, to_apply=%region_21.22 | all-reduce | flops 28672 | bytes 114688 | tf_op jit(solution)/shard_map/psum | solution.py:277
  455.2 11.9 %all_gather.16 = f32[8,2048]{1,0:T(8,128)S(1)} all-gather(f32[8,512]{1,0:T(8,128)S(1)} %convert_element_type.314), channel_id=1, replica_groups=mesh['seq'=32,'tp'=4] {'tp'}, dimensions={1}, use_global_device_ids=true | all-gather | bytes 81920 | tf_op jit(solution)/shard_map/all_gather | solution.py:280
  468.3 2.2 convolution_reduce_fusion
  (275 shorter events, 91.0 us)
Async XLA Ops:
  7.2 190.1 %copy-start = (bf16[512,2048]{1,0:T(8,128)(2,1)S(1)}, bf16[512,2048]{1,0:T(8,128)(2,1)}, u32[]{:S(2)}) copy-start(bf16[512,2048]{1,0:T(8,128)(2,1)} %param.31) | copy-start | bytes 6291460
  7.2 93.8 %all-gather.5.cloned.1.call-start = ((), (), s32[]{:S(2)}) async-start(), calls=%async_computation.3 | async-start | bytes 8650752 | tf_op jit(solution)/shard_map/all_gather | solution.py:17
  8.9 5.3 %copy-start.6 = (s32[8]{0:T(128)S(1)}, s32[8]{0:T(128)}, u32[]{:S(2)}) copy-start(s32[8]{0:T(128)} %param.34) | copy-start | bytes 100
  8.9 5.3 %copy-start.12 = (s32[8]{0:T(128)S(1)}, s32[8]{0:T(128)}, u32[]{:S(2)}) copy-start(s32[8]{0:T(128)} %param.35) | copy-start | bytes 100
  8.9 5.8 %copy-start.4 = (f32[4,1024]{1,0:T(4,128)S(1)}, f32[4,1024]{1,0:T(4,128)}, u32[]{:S(2)}) copy-start(f32[4,1024]{1,0:T(4,128)} %param.25) | copy-start | bytes 49156
  8.9 5.8 %copy-start.7 = (bf16[2048,16]{0,1:T(8,128)(2,1)S(1)}, bf16[2048,16]{0,1:T(8,128)(2,1)}, u32[]{:S(2)}) copy-start(bf16[2048,16]{0,1:T(8,128)(2,1)} %param.26) | copy-start | bytes 196612
  8.9 5.8 %copy-start.9 = (f32[2048]{0:T(1024)S(1)}, f32[2048]{0:T(1024)}, u32[]{:S(2)}) copy-start(f32[2048]{0:T(1024)} %param.23) | copy-start | bytes 24580
  8.9 7.5 %copy-start.8 = (bf16[16,256]{1,0:T(8,128)(2,1)S(1)}, bf16[16,256]{1,0:T(8,128)(2,1)}, u32[]{:S(2)}) copy-start(bf16[16,256]{1,0:T(8,128)(2,1)} %param.27) | copy-start | bytes 24580
  9.0 7.5 %copy-start.11 = (f32[256]{0:T(256)S(1)}, f32[256]{0:T(256)}, u32[]{:S(2)}) copy-start(f32[256]{0:T(256)} %param.28) | copy-start | bytes 3076
  12.9 5.3 %collective-permute-start = (bf16[3,1024]{1,0:T(4,128)(2,1)S(1)}, bf16[3,1024]{1,0:T(4,128)(2,1)S(1)}, u32[]{:S(2)}, u32[]{:S(2)}) collective-permute-start(bf16[3,1024]{1,0:T(4,128)(2,1)S(1)} %slice.111), channel_id=1, source_target_pairs={{0,4},{4,8},{8,12},{12,16},{16,20},{20,24},{24,28},{28,32},{32,36}... | collective-permute-start | bytes 18440 | tf_op jit(solution)/shard_map/ppermute | solution.py:40
  43.6 257.0 %all-reduce.3.cloned.1.call-start = ((), (), s32[]{:S(2)}) async-start(), calls=%async_computation.2 | async-start | bytes 4194304 | tf_op jit(solution)/shard_map/psum | solution.py:278
  193.3 1.0 copy-start.2
  193.3 1.2 copy-start.10
  193.3 133.2 %reduce-scatter.2.cloned.1.call-start = ((), (), s32[]{:S(2)}) async-start(), calls=%async_computation.1 | async-start | bytes 1310720 | tf_op jit(solution)/shard_map/reduce_scatter | solution.py:257
  199.0 2.9 copy-start.1
  203.9 264.4 %copy-start.5 = (f32[2048]{0:T(1024)S(1)}, f32[2048]{0:T(1024)}, u32[]{:S(2)}) copy-start(f32[2048]{0:T(1024)} %param.32) | copy-start | bytes 24580
  327.7 142.9 %copy-start.3 = (bf16[256,512]{1,0:T(8,128)(2,1)}, bf16[256,512]{1,0:T(8,128)(2,1)S(1)}, u32[]{:S(2)}) copy-start(bf16[256,512]{1,0:T(8,128)(2,1)S(1)} %add_convert_fusion) | copy-start | bytes 786436
Sparse Core Ops, SparseCore 0:
  43.7 57.1 all-gather.4
  193.4 107.1 all-reduce.2
  303.0 23.4 reduce-scatter.1
where the time goes:
time: 480 us; the launch traced here: 477 us
  blocking collectives  165 us (34%)
  waiting for transfers between devices  147 us (31%)
  other arithmetic  81.7 us (17%)
  matrix products  27.2 us (6%)
  local copies, waits for them, and re-layouts  24.3 us (5%)
  between operations  15.3 us (3%)
  loops' own time  14.8 us (3%)
    psum x1, blocking collectives, shards(): lax.psum(conv_edges.astype(jnp.bfloat16), 'seq').astype(jnp.float32)  127 us
    psum x1, waiting for transfers between devices, shards(): lax.psum(end_states.astype(jnp.bfloat16), 'seq').astype(jnp.float32)  96.7 us
    select_n x32, other arithmetic, hop(): return jax.tree.map(lambda a, b: jnp.where(reached, a, b), new, before)  34.9 us
    all_gather x1, waiting for transfers between devices, prefix(): lax.all_gather(part.astype(kind), axis)  29 us
    all_gather x1, blocking collectives, prefix(): lax.all_gather(part.astype(kind), axis)  26.3 us
    reduce_scatter x1, waiting for transfers between devices, shards(): lax.psum_scatter(projected_out.astype(jnp.bfloat16), 'tp', scatter_dimens...  21.7 us
    all_gather x1, blocking collectives, shards(): full_rows = lax.all_gather(row_sums, 'tp', axis=1, tiled=True)  11.9 us
    dynamic_slice x24, local copies, waits for them, and re-layouts, shards(): local_state, unused_steps = lax.scan(state_only, empty_state, block_inputs)  10.5 us
  transfers between devices with their start and end apart: 4, of which 3 were waited for; matrix products, arithmetic and copies ran while one was open for 4% of the time, Pallas kernels for 0%

commit v1 on v0

--- a/solution.py
+++ b/solution.py
@@ -196,6 +196,20 @@
     lengths,
     packed_order,
 ):
+
+    def rings_track(u_in, a_name):
+        fan = lax.axis_size(a_name)
+        sheets = [(m, (m + 1) % fan) for m in range(fan)]
+        items = [(m, (m - 1) % fan) for m in range(fan)]
+        top, x_now = ([u_in], [u_in])
+        for _ in range(fan // 2):
+            top.append(lax.ppermute(top[-1], a_name, sheets))
+        for _ in tuple(range((fan - 1) // 2)):
+            next_value = lax.ppermute(x_now[-1], a_name, items)
+            x_now.append(next_value)
+        tmp = jnp.concatenate([*top[::-1], *x_now[1:]], axis=1)
+        return jnp.roll(tmp, shift=(lax.axis_index(a_name) - fan // 2) * u_in.shape[1], axis=1)
+
     row_count = tokens.shape[0]
     head_count = out_weight.shape[0] // DV
     column_count = tokens.shape[1] // lax.axis_size("tp")
@@ -277,7 +291,7 @@
         lax.psum(conv_edges.astype(jnp.bfloat16), "seq").astype(jnp.float32),
         lax.psum(end_states.astype(jnp.bfloat16), "seq").astype(jnp.float32),
     )
-    full_rows = lax.all_gather(row_sums, "tp", axis=1, tiled=True)
+    full_rows = rings_track(row_sums, "tp")
     mean_square = jnp.mean(full_rows * full_rows, axis=1)
     last_norms = jnp.sqrt(mean_square)
     final_rows = (full_rows * lax.rsqrt(mean_square[:, None] + 1e-06) * final_gain).astype(

time: 480 us -> 377 us (0.79)
  waiting for transfers between devices: 147 us -> 50.3 us
  blocking collectives: 165 us -> 154 us
    psum x1, waiting for transfers between devices: 96.7 us -> 0.02 us  [shards(): lax.psum(end_states.astype(jnp.bfloat16), 'seq').astype(jnp.float32)]
    all_gather x1 -> x0, blocking collectives: 11.9 us -> none  [shards(): full_rows = lax.all_gather(row_sums, 'tp', axis=1, tiled=True)]
    ppermute x0 -> x3, waiting for transfers between devices: none -> 5.72 us  [the longest x2 4.95 us: rings_track(): top.append(lax.ppermute(top[-1], a_name, sheets))]
    reduce_scatter x1, waiting for transfers between devices: 21.7 us -> 16.2 us  [shards(): lax.psum_scatter(projected_out.astype(jnp.bfloat16), 'tp', scatter_dimens...]
  transfers between devices with their start and end apart: 4 -> 7, of which waited for: 3 -> 4; matrix products, arithmetic and copies ran while one was open for 4% -> 5% of each run, Pallas kernels for 0% -> 0%
where the time goes in v1:
time: 377 us; the launch traced here: 374 us
  blocking collectives  154 us (41%)
  other arithmetic  82.7 us (22%)
  waiting for transfers between devices  50.3 us (13%)
  local copies, waits for them, and re-layouts  27.5 us (7%)
  matrix products  24.9 us (7%)
  between operations  15.4 us (4%)
  loops' own time  14.8 us (4%)
  starting transfers between devices  4.63 us (1%)
    psum x1, blocking collectives, shards(): lax.psum(conv_edges.astype(jnp.bfloat16), 'seq').astype(jnp.float32)  127 us
    select_n x32, other arithmetic, hop(): return jax.tree.map(lambda a, b: jnp.where(reached, a, b), new, before)  34.9 us
    all_gather x1, waiting for transfers between devices, prefix(): lax.all_gather(part.astype(kind), axis)  28.3 us
    all_gather x1, blocking collectives, prefix(): lax.all_gather(part.astype(kind), axis)  27 us
    reduce_scatter x1, waiting for transfers between devices, shards(): lax.psum_scatter(projected_out.astype(jnp.bfloat16), 'tp', scatter_dimens...  16.2 us
    dynamic_slice x24, local copies, waits for them, and re-layouts, shards(): local_state, unused_steps = lax.scan(state_only, empty_state, block_inputs)  10.5 us
    another operation x1, loops' own time, shards(): lax.scan(stepper, (incoming, empty_ends), block_inputs)  8.27 us
    reduce_sum x4, other arithmetic, block_step(): jnp.sum(query_rows[:, None] * key_floats[None, :] * weights, axis=-1)  8.17 us
  transfers between devices with their start and end apart: 7, of which 4 were waited for; matrix products, arithmetic and copies ran while one was open for 5% of the time, Pallas kernels for 0%

profile of v1, /device:TPU:0, one launch (start us, length us, event | category | flops | bytes accessed | tf_op | source)
XLA Modules:
  0.0 374.3 jit_solution(11135848003077636718)
XLA Ops:
  7.2 1.6 multiply_reduce_fusion.1
  9.0 3.9 %convolution_convert_fusion.1 = bf16[256,1024]{1,0:T(8,128)(2,1)S(1)} fusion(bf16[2048,1024]{1,0:T(8,128)(2,1)} %param.24, f32[2048]{0:T(1024)} %param.23, f32[256]{0:T(256)S(1)} %add_rsqrt_fusion.1, bf16[256,2048]{1,0:T(8,128)(2,1)} %param.22), kind=kOutput, calls=%fused_computation.94 | convolution fusion | flops 1076101120 | bytes 5776384 | tf_op jit(solution)/shard_map/dot_general | solution.py:228
  13.7 1.3 collective-permute-start
  17.8 2.1 pad_maximum_fusion
  21.7 21.8 %while.43 = (s32[]{:T(128)}, f32[1,256,512]{2,1,0:T(8,128)S(1)}, s32[4,64]{1,0:T(4,128)S(1)}, s32[4]{0:T(128)S(1)}, f32[4,64,1,256]{3,2,1,0:T(1,128)}, /*index=5...) while((s32[]{:T(128)}, f32[1,256,512]{2,1,0:T(8,128)S(1)}, ...), condition=%wide.region_7.8_spmd.clone, body=%wide.region_5.7_spmd.clone.sunk | while | flops 18415684 | bytes 1417237 | solution.py:264
  26.0 1.2 fusion.124
  31.4 1.2 fusion.124
  36.9 1.2 fusion.124
  42.3 1.2 fusion.124
  46.2 27.0 %all-gather.2 = bf16[32,1,256]{2,1,0:T(2,128)(2,1)S(1)} all-gather(bf16[1,1,256]{2,1,0:T(2,128)(2,1)S(1)} %reshape.975), channel_id=2, replica_groups=mesh['seq'=32,'tp'=4] {'seq'}, dimensions={0}, use_global_device_ids=true | all-gather | bytes 16896 | tf_op jit(solution)/shard_map/all_gather | solution.py:17
  73.3 28.3 %all-gather.5.cloned.1.call-done = bf16[32,256,512]{2,1,0:T(8,128)(2,1)} async-done(((bf16[1,256,512]{2,1,0:T(8,128)(2,1)}), bf16[32,256,512]{2,1,0:T(8,128)(2,1)}) %all-gather.5.cloned.1.call-update) | async-done | bytes 8388624 | tf_op jit(solution)/shard_map/all_gather | solution.py:17
  101.6 36.2 %while.44 = (s32[]{:T(128)}, f32[1,256,512]{2,1,0:T(8,128)S(1)}, s32[]{:T(128)}, bf16[32,1,256]{2,1,0:T(2,128)(2,1)S(1)}, bf16[32,1,256,512]{3,2,1,0:T(8,128)(2,1)}, /*index=5*/s32[]{:T(128)}, s32[]{:T(128)}) while((s32[]{:T(128)}, f32[1,256,512]{2,1,0:T(8,128)S(1)}, s32[]{:T(128)}, bf16[32,1,256]{2,1,0:T(2,128)(2,1)S(1)}, ...), condition=%wide.region_9.10_spmd.clone, body=%wide.region_8.9_spmd.clone.sunk | while | flops 655620 | bytes 1313385 | solution.py:34
  137.8 1.5 broadcast_in_dim.240
  139.3 54.6 %while.42 = (s32[]{:T(128)}, f32[1,256,512]{2,1,0:T(8,128)S(1)}, bf16[8,1,256,512]{3,2,0,1:T(8,128)(2,1)}, f32[4,64,1,512]{3,1,2,0:T(8,128)}, s32[4,64]{1,0:T(4,...) while((s32[]{:T(128)}, f32[1,256,512]{2,1,0:T(8,128)S(1)}, ...), condition=%wide.region_17.18_spmd, body=%wide.region_11.17_spmd.sunk | while | flops 268659424 | bytes 8804605 | solution.py:267
  145.0 5.8 %conditional.2 = (bf16[8,1,256,512]{3,2,0,1:T(8,128)(2,1)}) conditional(s32[]{:T(128)} %convert_element_type.390, bf16[8,1,256,512]{3,2,0,1:T(8,128)(2,1)} %get-tuple-element.722, (pred[8]{0:T(512)(128)(4,1)S(1)}, s32[8]{0:T(128)S(1)}, s32[64]{0:T(128)S(1)}, bf16[1,64,1,256]{3,2,1,0:T(2,128)(2,1)S(1)}, f32[64,1,256]{2,1,0:T(1,128)S(1)}, ...), branch_computations={%region_14.14_spmd, %region_15.15_spmd} | conditional | flops 139086368 | bytes 5199492 | solution.py:107
  147.0 3.7 fusion
  150.9 2.0 multiply_reduce_fusion.5
  163.2 2.0 multiply_reduce_fusion.5
  175.4 2.0 multiply_reduce_fusion.5
  187.6 2.0 multiply_reduce_fusion.5
  195.1 2.9 fusion.56
  198.0 1.7 convolution_convert_fusion
  199.9 1.6 convert_element_type.287
  201.5 1.7 gather_fusion.4
  203.2 1.7 gather_fusion.3
  204.9 1.7 gather_fusion.2
  206.9 16.2 %reduce-scatter.2.cloned.1.call-done = bf16[256,512]{1,0:T(8,128)(2,1)} async-done(((bf16[256,2048]{1,0:T(8,128)(2,1)}), bf16[256,512]{1,0:T(8,128)(2,1)}) %reduce-scatter.2.cloned.1.call-update) | async-done | bytes 262160 | tf_op jit(solution)/shard_map/reduce_scatter | solution.py:271
  223.1 1.2 add_convert_fusion
  224.9 127.2 %all-reduce = (bf16[8,3,1024]{2,0,1:T(8,128)(2,1)S(1)}, bf16[8,512]{1,0:T(8,128)(2,1)S(1)}) all-reduce(bf16[8,3,1024]{2,0,1:T(8,128)(2,1)S(1)} %pad_maximum_fusion.1, bf16[8,512]{1,0:T(8,128)(2,1)S(1)} %select_convert_fusion.2), channel_id=1, replica_groups=mesh['seq'=32,'tp'=4] {'seq'}, use_global_device_ids=true, to_apply=%region_21.22 | all-reduce | flops 28672 | bytes 114688 | tf_op jit(solution)/shard_map/psum | solution.py:291
  352.2 4.9 %collective-permute-done.1 = f32[8,512]{1,0:T(8,128)S(1)} collective-permute-done((f32[8,512]{1,0:T(8,128)S(1)}, f32[8,512]{1,0:T(8,128)S(1)}, u32[]{:S(2)}, u32[]{:S(2)}) %collective-permute-start.1) | collective-permute-done | bytes 16416 | tf_op jit(solution)/shard_map/ppermute | solution.py:206
  357.1 4.3 %convert_element_type.304 = f32[8,1,256,512]{3,2,1,0:T(8,128)} convert(bf16[8,1,256,512]{3,2,1,0:T(8,128)(2,1)} %all-reduce.3.cloned.1.call-done) | non-fusion elementwise | flops 1048576 | bytes 6291456 | tf_op jit(solution)/shard_map/convert_element_type | solution.py:292
  361.4 3.2 collective-permute-start.3
  (292 shorter events, 93.6 us)
Async XLA Ops:
  7.2 190.8 %copy-start = (bf16[512,2048]{1,0:T(8,128)(2,1)S(1)}, bf16[512,2048]{1,0:T(8,128)(2,1)}, u32[]{:S(2)}) copy-start(bf16[512,2048]{1,0:T(8,128)(2,1)} %param.31) | copy-start | bytes 6291460
  7.2 94.4 %all-gather.5.cloned.1.call-start = ((), (), s32[]{:S(2)}) async-start(), calls=%async_computation.3 | async-start | bytes 8650752 | tf_op jit(solution)/shard_map/all_gather | solution.py:17
  8.9 6.1 %copy-start.8 = (s32[8]{0:T(128)S(1)}, s32[8]{0:T(128)}, u32[]{:S(2)}) copy-start(s32[8]{0:T(128)} %param.34) | copy-start | bytes 100
  8.9 6.1 %copy-start.14 = (s32[8]{0:T(128)S(1)}, s32[8]{0:T(128)}, u32[]{:S(2)}) copy-start(s32[8]{0:T(128)} %param.35) | copy-start | bytes 100
  8.9 6.7 %copy-start.6 = (f32[4,1024]{1,0:T(4,128)S(1)}, f32[4,1024]{1,0:T(4,128)}, u32[]{:S(2)}) copy-start(f32[4,1024]{1,0:T(4,128)} %param.25) | copy-start | bytes 49156
  8.9 6.7 %copy-start.1 = (bf16[256,2048]{1,0:T(8,128)(2,1)S(1)}, bf16[256,2048]{1,0:T(8,128)(2,1)}, u32[]{:S(2)}) copy-start(bf16[256,2048]{1,0:T(8,128)(2,1)} %param.22) | copy-start | bytes 3145732
  8.9 6.7 %copy-start.9 = (bf16[2048,16]{0,1:T(8,128)(2,1)S(1)}, bf16[2048,16]{0,1:T(8,128)(2,1)}, u32[]{:S(2)}) copy-start(bf16[2048,16]{0,1:T(8,128)(2,1)} %param.26) | copy-start | bytes 196612
  8.9 6.7 %copy-start.11 = (f32[2048]{0:T(1024)S(1)}, f32[2048]{0:T(1024)}, u32[]{:S(2)}) copy-start(f32[2048]{0:T(1024)} %param.23) | copy-start | bytes 24580
  9.0 7.1 %copy-start.10 = (bf16[16,256]{1,0:T(8,128)(2,1)S(1)}, bf16[16,256]{1,0:T(8,128)(2,1)}, u32[]{:S(2)}) copy-start(bf16[16,256]{1,0:T(8,128)(2,1)} %param.27) | copy-start | bytes 24580
  9.0 7.1 %copy-start.13 = (f32[256]{0:T(256)S(1)}, f32[256]{0:T(256)}, u32[]{:S(2)}) copy-start(f32[256]{0:T(256)} %param.28) | copy-start | bytes 3076
  12.9 0.8 copy-start.4
  13.7 4.1 %collective-permute-start = (bf16[3,1024]{1,0:T(4,128)(2,1)S(1)}, bf16[3,1024]{1,0:T(4,128)(2,1)S(1)}, u32[]{:S(2)}, u32[]{:S(2)}) collective-permute-start(bf16[3,1024]{1,0:T(4,128)(2,1)S(1)} %slice.111), channel_id=1, source_target_pairs={{0,4},{4,8},{8,12},{12,16},{16,20},{20,24},{24,28},{28,32},{32,36}... | collective-permute-start | bytes 18440 | tf_op jit(solution)/shard_map/ppermute | solution.py:40
  44.3 178.8 %reduce-scatter.2.cloned.1.call-start = ((), (), s32[]{:S(2)}) async-start(), calls=%async_computation.1 | async-start | bytes 1310720 | tf_op jit(solution)/shard_map/reduce_scatter | solution.py:271
  139.3 55.9 %copy-start.12 = (f32[512]{0:T(512)S(1)}, f32[512]{0:T(512)}, u32[]{:S(2)}) copy-start(f32[512]{0:T(512)} %param.30) | copy-start | bytes 6148
  198.0 1.8 copy-start.2
  199.8 157.3 %all-reduce.3.cloned.1.call-start = ((), (), s32[]{:S(2)}) async-start(), calls=%async_computation.2 | async-start | bytes 4194304 | tf_op jit(solution)/shard_map/psum | solution.py:292
  224.3 137.1 %copy-start.5 = (bf16[256,512]{1,0:T(8,128)(2,1)}, bf16[256,512]{1,0:T(8,128)(2,1)S(1)}, u32[]{:S(2)}) copy-start(bf16[256,512]{1,0:T(8,128)(2,1)S(1)} %add_convert_fusion) | copy-start | bytes 786436
  352.2 4.9 %collective-permute-start.1 = (f32[8,512]{1,0:T(8,128)S(1)}, f32[8,512]{1,0:T(8,128)S(1)}, u32[]{:S(2)}, u32[]{:S(2)}) collective-permute-start(f32[8,512]{1,0:T(8,128)S(1)} %convert_element_type.314), channel_id=1, source_target_pairs={{0,1},{1,2},{2,3},{3,0},{4,5},{5,6},{6,7},{7,4},{8,9},{9,10},{10,1... | collective-permute-start | bytes 49160 | tf_op jit(solution)/shard_map/ppermute | solution.py:206
  357.1 8.2 %collective-permute-start.2 = (f32[8,512]{1,0:T(8,128)S(1)}, f32[8,512]{1,0:T(8,128)S(1)}, u32[]{:S(2)}, u32[]{:S(2)}) collective-permute-start(f32[8,512]{1,0:T(8,128)S(1)} %collective-permute-done.1), channel_id=1, source_target_pairs={{0,1},{1,2},{2,3},{3,0},{4,5},{5,6},{6,7},{7,4},{8,9},{9,10},{10,1... | collective-permute-start | bytes 49160 | tf_op jit(solution)/shard_map/ppermute | solution.py:206
  357.1 9.6 %copy-start.3 = (bf16[250,2048]{1,0:T(8,128)(2,1)S(1)}, bf16[250,2048]{1,0:T(8,128)(2,1)}, u32[]{:S(2)}) copy-start(bf16[250,2048]{1,0:T(8,128)(2,1)} %param.33) | copy-start | bytes 3072004
  357.1 9.6 %copy-start.7 = (f32[2048]{0:T(1024)S(1)}, f32[2048]{0:T(1024)}, u32[]{:S(2)}) copy-start(f32[2048]{0:T(1024)} %param.32) | copy-start | bytes 24580
  361.4 4.7 %collective-permute-start.3 = (f32[8,512]{1,0:T(8,128)S(1)}, f32[8,512]{1,0:T(8,128)S(1)}, u32[]{:S(2)}, u32[]{:S(2)}) collective-permute-start(f32[8,512]{1,0:T(8,128)S(1)} %convert_element_type.314), channel_id=1, source_target_pairs={{0,3},{1,0},{2,1},{3,2},{4,7},{5,4},{6,5},{7,6},{8,11},{9,8},{10,9... | collective-permute-start | bytes 49160 | tf_op jit(solution)/shard_map/ppermute | solution.py:208
Sparse Core Ops, SparseCore 0:
  44.4 57.1 all-gather.4
  199.9 23.1 reduce-scatter.1
  226.9 107.3 all-reduce.2
